TPU v7x, 512 devices: a whole 4x8x8 slice. The times are simulated.
512 devices in a mesh: dp: 32 (over z, y_lo, core), feat: 16 (over y_hi, x).
Axes of the slice: x: 4, y: 8 (y_hi: 4, y_lo: 2; y = y_hi * 2 + y_lo), z: 8, core: 2. Of those that a mesh axis runs over, the one named last changes fastest.
Arguments:
- tokens: bfloat16 [8192, 8192], P('dp', 'feat'), may hold values from -6 to 6
- up_left: bfloat16 [16, 512, 2048], P('feat', 'dp'), may hold values from -0.25 to 0.25
- up_right: bfloat16 [2048, 16, 16], P('feat'), may hold values from -1.5 to 1.5
- down_left: bfloat16 [16, 2048, 512], P('feat', 'dp'), may hold values from -0.125 to 0.125
- down_right: bfloat16 [512, 16, 16], P('feat'), may hold values from -1.5 to 1.5
- layer_grad: bfloat16 [8192, 8192], P('dp', 'feat'), may hold values from -6 to 6
Outputs:
- layer_out: bfloat16 [8192, 8192], P('dp', 'feat')
- grad_tokens: bfloat16 [8192, 8192], P('dp', 'feat')
- grad_up_left: float32 [16, 512, 2048], P('feat', 'dp')
- grad_up_right: float32 [2048, 16, 16], P('feat')
- grad_down_left: float32 [16, 2048, 512], P('feat', 'dp')
- grad_down_right: float32 [512, 16, 16], P('feat')
All inputs are finite; a program needn't handle non-finite values.
Results may differ from a plain program's by a relative error of at most 0.0067.
Values may be sent and summed in bfloat16 or wider, within the bound.
No kernel may reach another device: no remote copies, remote signals or barrier semaphores. Data moves between devices by JAX's collectives and lax.ppermute only.
A program may use at most 128 MiB of HBM per device.

v0:
```python
import jax
import jax.numpy as jnp
import numpy as np
from jax import lax
from jax.sharding import Mesh
from jax.sharding import PartitionSpec as P

TILE_UP = 128
TILE_DOWN = 32
DP_AXES = ("z", "ylo", "core")
FEAT_AXES = ("yhi", "x")


def split_mesh(mesh):
    n_dp = mesh.shape["dp"]
    n_feat = mesh.shape["feat"]
    sizes = (n_dp // 4, 2, 2, n_feat // 4, 4)
    devices = np.asarray(mesh.devices).reshape(sizes)
    return Mesh(devices, DP_AXES + FEAT_AXES)


def exchange(wired):
    rows, feat_count, piece = wired.shape
    n_x = lax.axis_size("x")
    n_y = feat_count // n_x
    shaped = wired.reshape(rows, n_y, n_x, piece)
    shaped = lax.all_to_all(shaped, "x", 2, 2, tiled=True)
    shaped = lax.all_to_all(shaped, "yhi", 1, 1, tiled=True)
    return shaped.reshape(rows, feat_count, piece)


def dp_reduce_scatter(part, row_axis):
    shape = part.shape
    rows = shape[row_axis]
    n_z = lax.axis_size("z")
    split = shape[:row_axis] + (n_z, 2, 2, rows // (4 * n_z)) + shape[row_axis + 1 :]
    x = part.reshape(split)
    x = lax.psum_scatter(x, "core", scatter_dimension=row_axis + 2, tiled=True)
    x = lax.psum_scatter(x, "z", scatter_dimension=row_axis, tiled=True)
    x = lax.psum_scatter(x, "ylo", scatter_dimension=row_axis + 1, tiled=True)
    return x.reshape(shape[:row_axis] + (rows // (4 * n_z),) + shape[row_axis + 1 :])


def dp_all_gather(local, row_axis):
    shape = local.shape
    rows = shape[row_axis]
    x = local.reshape(shape[:row_axis] + (1, 1, 1, rows) + shape[row_axis + 1 :])
    x = lax.all_gather(x, "ylo", axis=row_axis + 1, tiled=True)
    x = lax.all_gather(x, "z", axis=row_axis, tiled=True)
    x = lax.all_gather(x, "core", axis=row_axis + 2, tiled=True)
    total = x.shape[row_axis] * x.shape[row_axis + 1] * x.shape[row_axis + 2] * rows
    return x.reshape(shape[:row_axis] + (total,) + shape[row_axis + 1 :])


def to_wire(blocks, feat_count):
    tok_rows, local_blocks, full_width = blocks.shape
    piece = full_width // feat_count
    shaped = blocks.reshape(tok_rows, local_blocks, feat_count, piece).transpose(0, 2, 1, 3)
    return shaped.reshape(tok_rows, feat_count, local_blocks * piece)


def from_wire(wired, local_blocks):
    tok_rows, feat_count, line_len = wired.shape
    piece = line_len // local_blocks
    shaped = wired.reshape(tok_rows, feat_count, local_blocks, piece).transpose(0, 2, 1, 3)
    return shaped.reshape(tok_rows, local_blocks, feat_count * piece)


def on_device(tokens, up_left, up_right, down_left, down_right, layer_grad):
    tok_rows = tokens.shape[0]
    local_blocks = up_left.shape[0]
    hidden_width = up_left.shape[2]
    block_width = down_left.shape[2]
    blocks_all = up_right.shape[1]
    group_up = up_right.shape[0]
    group_down = down_right.shape[0]
    feat_count = lax.axis_size("yhi") * lax.axis_size("x")
    n_dp = lax.axis_size("z") * lax.axis_size("ylo") * lax.axis_size("core")
    grad_scale = float(tok_rows * n_dp) ** (-0.5)
    tiles_up = group_up // TILE_UP
    tiles_down = group_down // TILE_DOWN
    up_full = dp_all_gather(up_left, 1)
    token_blocks = tokens.reshape(tok_rows, local_blocks, block_width)
    up_inner = jnp.einsum(
        "tbi,big->tbg", token_blocks, up_full, preferred_element_type=jnp.float32
    ).astype(jnp.bfloat16)
    up_mixed = exchange(to_wire(up_inner, feat_count))
    preact = jnp.einsum("tjg,gjk->tkg", up_mixed, up_right, preferred_element_type=jnp.float32)
    sigmoid_val = jax.nn.sigmoid(preact)
    activated = (
        (preact * sigmoid_val)
        .reshape(tok_rows, blocks_all, tiles_up, TILE_UP)
        .transpose(0, 2, 1, 3)
    )
    hidden = activated.reshape(tok_rows, local_blocks, hidden_width).astype(jnp.bfloat16)
    down_full = dp_all_gather(down_left, 1)
    down_inner = jnp.einsum(
        "tbh,bhc->tbc", hidden, down_full, preferred_element_type=jnp.float32
    ).astype(jnp.bfloat16)
    down_mixed = exchange(to_wire(down_inner, feat_count)).reshape(
        tok_rows, blocks_all * group_down
    )
    identity = jnp.eye(group_down, dtype=jnp.bfloat16).reshape(group_down, tiles_down, TILE_DOWN)
    mix_matrix = jnp.einsum(
        "cjk,cal->jcakl", down_right, identity, preferred_element_type=jnp.float32
    )
    mix_matrix = mix_matrix.astype(jnp.bfloat16).reshape(
        blocks_all * group_down, blocks_all * group_down
    )
    layer_out = jnp.dot(down_mixed, mix_matrix, preferred_element_type=jnp.float32).astype(
        jnp.bfloat16
    )
    grad_down_mixed = lax.dot_general(
        layer_grad, mix_matrix, (((1,), (1,)), ((), ())), preferred_element_type=jnp.float32
    ).astype(jnp.bfloat16)
    grad_by_group = layer_grad.reshape(tok_rows, tiles_down, blocks_all, TILE_DOWN).transpose(
        0, 2, 1, 3
    )
    grad_by_group = grad_by_group.reshape(tok_rows, blocks_all, group_down)
    right_down_term = (
        jnp.einsum(
            "tjc,tkc->cjk",
            down_mixed.reshape(tok_rows, blocks_all, group_down),
            grad_by_group,
            preferred_element_type=jnp.float32,
        )
        * grad_scale
    )
    grad_down_inner = from_wire(
        exchange(grad_down_mixed.reshape(tok_rows, feat_count, local_blocks * group_down)),
        local_blocks,
    )
    grad_down_left = dp_reduce_scatter(
        jnp.einsum("tbh,tbc->hbc", hidden, grad_down_inner, preferred_element_type=jnp.float32)
        * grad_scale,
        0,
    ).transpose(1, 0, 2)
    grad_hidden = jnp.einsum(
        "tbc,bhc->tbh", grad_down_inner, down_full, preferred_element_type=jnp.float32
    )
    grad_hidden = grad_hidden.reshape(tok_rows, tiles_up, blocks_all, TILE_UP).transpose(0, 2, 1, 3)
    grad_hidden = grad_hidden.reshape(tok_rows, blocks_all, group_up)
    grad_preact = (grad_hidden * sigmoid_val * (1.0 + preact * (1.0 - sigmoid_val))).astype(
        jnp.bfloat16
    )
    grad_up_mixed = jnp.einsum(
        "tkg,gjk->tjg", grad_preact, up_right, preferred_element_type=jnp.float32
    ).astype(jnp.bfloat16)
    right_up_term = (
        jnp.einsum("tjg,tkg->gjk", up_mixed, grad_preact, preferred_element_type=jnp.float32)
        * grad_scale
    )
    grad_up_inner = from_wire(exchange(grad_up_mixed), local_blocks)
    grad_tokens = jnp.einsum(
        "tbg,big->tbi", grad_up_inner, up_full, preferred_element_type=jnp.float32
    ).astype(jnp.bfloat16)
    grad_tokens = grad_tokens.reshape(tok_rows, local_blocks * block_width)
    grad_up_left = dp_reduce_scatter(
        jnp.einsum("tbi,tbg->ibg", token_blocks, grad_up_inner, preferred_element_type=jnp.float32)
        * grad_scale,
        0,
    ).transpose(1, 0, 2)
    rights = jnp.concatenate([right_up_term, right_down_term], axis=0)
    rights = lax.psum(rights, DP_AXES)
    grad_up_right = rights[:group_up]
    grad_down_right = rights[group_up:]
    return (layer_out, grad_tokens, grad_up_left, grad_up_right, grad_down_left, grad_down_right)


def solution(mesh):
    fine = split_mesh(mesh)
    row = P(DP_AXES, FEAT_AXES)
    weight = P(FEAT_AXES, DP_AXES, None)
    mixer = P(FEAT_AXES, None, None)
    return jax.shard_map(
        on_device,
        mesh=fine,
        in_specs=(row, weight, mixer, weight, mixer, row),
        out_specs=(row, row, weight, mixer, weight, mixer),
        check_vma=False,
    )
```

profile of v0, /device:TPU:1, one launch (start us, length us, event | category | flops | bytes accessed | tf_op | source)
XLA Modules:
  0.0 650.3 jit_solution(2913419054008153790)
XLA Ops:
  7.2 6.3 all-gather
  13.6 42.4 %all-gather.13.cloned.1.call-done = bf16[16,16,2048]{2,1,0:T(8,128)(2,1)} async-done(((bf16[2,16,2048]{2,1,0:T(8,128)(2,1)}), bf16[16,16,2048]{2,1,0:T(8,128)(2,1)}) %all-gather.13.cloned.1.call-update) | async-done | bytes 1048592 | tf_op jit(solution)/shard_map/all_gather | solution.py:49
  56.1 5.3 all-gather.2
  70.8 10.1 %all-gather.9.cloned.1.call-done = bf16[1,8,2,2,16,2048]{5,4,3,2,1,0:T(8,128)(2,1)} async-done(((bf16[1,8,2,1,16,2048]{5,4,3,2,1,0:T(8,128)(2,1)}), bf16[1,8,2,2,16,2048]{5,4,3,2,1,0:T(8,128)(2,1)}) %all-gather.9.cloned.1.call-update) | async-done | bytes 2097168 | tf_op jit(solution)/shard_map/all_gather | solution.py:50
  87.9 32.6 %all-gather.15.cloned.1.call-done = bf16[16,64,512]{2,1,0:T(8,128)(2,1)} async-done(((bf16[2,64,512]{2,1,0:T(8,128)(2,1)}), bf16[16,64,512]{2,1,0:T(8,128)(2,1)}) %all-gather.15.cloned.1.call-update) | async-done | bytes 1048592 | tf_op jit(solution)/shard_map/all_gather | solution.py:49
  121.3 6.5 all-to-all-start.5
  128.8 6.9 %all-to-all-done.5 = bf16[256,4,4,32]{0,3,2,1:T(8,128)(2,1)S(1)} async-done(((bf16[256,4,4,32]{0,3,2,1:T(8,128)(2,1)}), bf16[256,4,4,32]{0,3,2,1:T(8,128)(2,1)S(1)}, u32[]{:S(2)}, u32[]{:S(2)}) %all-to-all-start.5) | async-done | bytes 262176 | tf_op jit(solution)/shard_map/all_to_all | solution.py:28
  135.7 4.3 all-to-all-start.1
  141.2 4.1 all-gather.11.cloned.1.call-done
  147.6 18.1 %all-to-all-done.1 = bf16[256,4,4,128]{0,3,2,1:T(8,128)(2,1)} async-done(((bf16[256,4,4,128]{0,3,2,1:T(8,128)(2,1)}), bf16[256,4,4,128]{0,3,2,1:T(8,128)(2,1)}, u32[]{:S(2)}, u32[]{:S(2)}) %all-to-all-start.1) | async-done | bytes 1048608 | tf_op jit(solution)/shard_map/all_to_all | solution.py:28
  165.8 4.5 fusion.7
  172.3 15.0 %all_to_all.40 = bf16[256,4,4,128]{0,3,1,2:T(8,128)(2,1)S(1)} all-to-all(bf16[256,4,4,128]{0,3,1,2:T(8,128)(2,1)S(1)} %copy.95), channel_id=1, replica_groups=mesh['z'=8,'ylo'=2,'core'=2,'yhi'=4,'x'=4] {'x'}, dimensions={2} | all-to-all | bytes 2097152 | tf_op jit(solution)/shard_map/all_to_all | solution.py:27
  188.4 6.5 %all-to-all-start.7 = ((bf16[256,4,4,128]{0,3,2,1:T(8,128)(2,1)}), bf16[256,4,4,128]{0,3,2,1:T(8,128)(2,1)S(1)}, u32[]{:S(2)}, u32[]{:S(2)}) async-start(bf16[256,4,4,128]{0,3,2,1:T(8,128)(2,1)} %copy.96), calls=%async_computation.7 | async-start | bytes 2097152 | tf_op jit(solution)/shard_map/all_to_all | solution.py:28
  199.0 5.4 copy.103
  204.5 10.2 %all-to-all-done.7 = bf16[256,4,4,128]{0,3,2,1:T(8,128)(2,1)S(1)} async-done(((bf16[256,4,4,128]{0,3,2,1:T(8,128)(2,1)}), bf16[256,4,4,128]{0,3,2,1:T(8,128)(2,1)S(1)}, u32[]{:S(2)}, u32[]{:S(2)}) %all-to-all-start.7) | async-done | bytes 1048608 | tf_op jit(solution)/shard_map/all_to_all | solution.py:28
  218.7 53.0 %all-reduce.8.cloned.1.call-done = (f32[8,2,2,16,1,2048]{5,3,4,2,1,0:T(8,128)}, f32[8,2,2,64,1,512]{5,3,2,1,0,4:T(8,128)}) async-done(((f32[8,2,2,16,1,2048]{5,3,4,2,1,0:T(8,128)}, f32[8,2,2,64,1,512]{5,3,2,1,0,4:T(8,128)}), (f32[8,2,2,16,1,2048]{5,3,4,2,1,0:T(8,128)}, f32[8,2,2,64,1,512]{5,3,2,1,0,4:T(8,128)})) %all-reduce.8.cloned.1.call-update) | async-done | bytes 8388624
  283.2 9.2 %all_to_all.41 = bf16[256,4,4,32]{0,3,1,2:T(8,128)(2,1)S(1)} all-to-all(bf16[256,4,4,32]{0,3,1,2:T(8,128)(2,1)S(1)} %copy.87), channel_id=1, replica_groups=mesh['z'=8,'ylo'=2,'core'=2,'yhi'=4,'x'=4] {'x'}, dimensions={2} | all-to-all | bytes 524288 | tf_op jit(solution)/shard_map/all_to_all | solution.py:27
  293.1 6.5 all-to-all-start.3
  302.9 5.1 all-to-all-done.3
  309.3 7.6 %reduce-scatter.13.cloned.1.call-done = f32[1,2,1,64,1,512]{5,3,2,1,0,4:T(8,128)} async-done(((f32[8,2,1,64,1,512]{5,3,2,1,0,4:T(8,128)}), f32[1,2,1,64,1,512]{5,3,2,1,0,4:T(8,128)}) %reduce-scatter.13.cloned.1.call-update) | async-done | bytes 262160 | tf_op jit(solution)/shard_map/reduce_scatter | solution.py:39
  317.0 46.2 %reduce-scatter.9.cloned.1.call-done = f32[1,2,1,16,1,2048]{5,3,4,2,1,0:T(8,128)} async-done(((f32[8,2,1,16,1,2048]{5,3,4,2,1,0:T(8,128)}), f32[1,2,1,16,1,2048]{5,3,4,2,1,0:T(8,128)}) %reduce-scatter.9.cloned.1.call-update) | async-done | bytes 262160 | tf_op jit(solution)/shard_map/reduce_scatter | solution.py:39
  364.3 233.1 %all-reduce.6.cloned.1.call-done = f32[160,16,16]{0,2,1:T(8,128)} async-done(((f32[160,16,16]{0,2,1:T(8,128)}), f32[160,16,16]{0,2,1:T(8,128)}) %all-reduce.6.cloned.1.call-update) | async-done | bytes 163856 | tf_op jit(solution)/shard_map/psum | solution.py:164
  603.6 16.7 %reduce-scatter.15.cloned.1.call-done = f32[1,1,1,64,1,512]{5,3,2,1,0,4:T(8,128)} async-done(((f32[1,2,1,64,1,512]{5,3,2,1,0,4:T(8,128)}), f32[1,1,1,64,1,512]{5,3,2,1,0,4:T(8,128)}) %reduce-scatter.15.cloned.1.call-update) | async-done | bytes 131088 | tf_op jit(solution)/shard_map/reduce_scatter | solution.py:40
  620.3 23.2 %reduce-scatter.11.cloned.1.call-done = f32[1,1,1,16,1,2048]{5,3,4,2,1,0:T(8,128)} async-done(((f32[1,2,1,16,1,2048]{5,3,4,2,1,0:T(8,128)}), f32[1,1,1,16,1,2048]{5,3,4,2,1,0:T(8,128)}) %reduce-scatter.11.cloned.1.call-update) | async-done | bytes 131088 | tf_op jit(solution)/shard_map/reduce_scatter | solution.py:40
  (84 shorter events, 57.2 us)
Async XLA Ops:
  7.2 73.8 %copy-start = (bf16[256,512]{1,0:T(8,128)(2,1)S(1)}, bf16[256,512]{1,0:T(8,128)(2,1)}, u32[]{:S(2)}) copy-start(bf16[256,512]{1,0:T(8,128)(2,1)} %param.6) | copy-start | bytes 786436
  7.2 48.8 %all-gather.13.cloned.1.call-start = ((), (), s32[]{:S(2)}) async-start(), calls=%async_computation.19 | async-start | bytes 1179648 | tf_op jit(solution)/shard_map/all_gather | solution.py:49
  13.6 67.3 %all-gather.9.cloned.1.call-start = ((), (), s32[]{:S(2)}) async-start(), calls=%async_computation.12 | async-start | bytes 3145728 | tf_op jit(solution)/shard_map/all_gather | solution.py:50
  56.0 64.5 %all-gather.15.cloned.1.call-start = ((), (), s32[]{:S(2)}) async-start(), calls=%async_computation.20 | async-start | bytes 1179648 | tf_op jit(solution)/shard_map/all_gather | solution.py:49
  62.3 3.5 copy-start.9
  66.9 17.5 %all-to-all-start.4 = ((bf16[256,4,4,32]{0,3,1,2:T(8,128)(2,1)}), bf16[256,4,4,32]{0,3,1,2:T(8,128)(2,1)S(1)}, u32[]{:S(2)}, u32[]{:S(2)}) async-start(bf16[256,4,4,32]{0,3,1,2:T(8,128)(2,1)} %copy.90), calls=%async_computation.4 | async-start | bytes 524288 | tf_op jit(solution)/shard_map/all_to_all | solution.py:27
  84.4 37.0 %all-to-all-start = ((bf16[256,4,4,128]{0,3,1,2:T(8,128)(2,1)}), bf16[256,4,4,128]{0,3,1,2:T(8,128)(2,1)S(1)}, u32[]{:S(2)}, u32[]{:S(2)}) async-start(bf16[256,4,4,128]{0,3,1,2:T(8,128)(2,1)} %copy.81), calls=%async_computation | async-start | bytes 2097152 | tf_op jit(solution)/shard_map/all_to_all | solution.py:27
  87.9 57.4 %all-gather.11.cloned.1.call-start = ((), (), s32[]{:S(2)}) async-start(), calls=%async_computation.13 | async-start | bytes 3145728 | tf_op jit(solution)/shard_map/all_gather | solution.py:50
  121.3 14.4 %all-to-all-start.5 = ((bf16[256,4,4,32]{0,3,2,1:T(8,128)(2,1)}), bf16[256,4,4,32]{0,3,2,1:T(8,128)(2,1)S(1)}, u32[]{:S(2)}, u32[]{:S(2)}) async-start(bf16[256,4,4,32]{0,3,2,1:T(8,128)(2,1)} %copy.91), calls=%async_computation.5 | async-start | bytes 524288 | tf_op jit(solution)/shard_map/all_to_all | solution.py:28
  127.8 12.2 %copy-start.11 = (bf16[128,16,16]{0,2,1:T(8,128)(2,1)S(1)}, bf16[128,16,16]{0,2,1:T(8,128)(2,1)}, u32[]{:S(2)}) copy-start(bf16[128,16,16]{0,2,1:T(8,128)(2,1)} %param.8) | copy-start | bytes 196612
  135.7 30.0 %all-to-all-start.1 = ((bf16[256,4,4,128]{0,3,2,1:T(8,128)(2,1)}), bf16[256,4,4,128]{0,3,2,1:T(8,128)(2,1)}, u32[]{:S(2)}, u32[]{:S(2)}) async-start(bf16[256,4,4,128]{0,3,2,1:T(8,128)(2,1)} %copy.82), calls=%async_computation.1 | async-start | bytes 2097152 | tf_op jit(solution)/shard_map/all_to_all | solution.py:28
  165.7 5.5 copy-start.7
  187.3 7.6 %copy-start.8 = (bf16[256,16,128]{0,1,2:T(8,128)(2,1)S(1)}, bf16[256,16,128]{0,1,2:T(8,128)(2,1)}, u32[]{:S(2)}) copy-start(bf16[256,16,128]{0,1,2:T(8,128)(2,1)} %get-tuple-element.21) | copy-start | bytes 3145732
  188.4 26.3 %all-to-all-start.7 = ((bf16[256,4,4,128]{0,3,2,1:T(8,128)(2,1)}), bf16[256,4,4,128]{0,3,2,1:T(8,128)(2,1)S(1)}, u32[]{:S(2)}, u32[]{:S(2)}) async-start(bf16[256,4,4,128]{0,3,2,1:T(8,128)(2,1)} %copy.96), calls=%async_computation.7 | async-start | bytes 2097152 | tf_op jit(solution)/shard_map/all_to_all | solution.py:28
  194.9 76.8 %all-reduce.8.cloned.1.call-start = ((), (), s32[]{:S(2)}) async-start(), calls=%async_computation.21 | async-start | bytes 16777216
  217.4 99.6 %reduce-scatter.13.cloned.1.call-start = ((), (), s32[]{:S(2)}) async-start(), calls=%async_computation.17 | async-start | bytes 2359296 | tf_op jit(solution)/shard_map/reduce_scatter | solution.py:39
  275.6 87.7 %reduce-scatter.9.cloned.1.call-start = ((), (), s32[]{:S(2)}) async-start(), calls=%async_computation.14 | async-start | bytes 2359296 | tf_op jit(solution)/shard_map/reduce_scatter | solution.py:39
  283.1 17.4 %copy-start.3 = (bf16[256,16,128]{0,1,2:T(8,128)(2,1)S(1)}, bf16[256,16,128]{0,1,2:T(8,128)(2,1)}, u32[]{:S(2)}) copy-start(bf16[256,16,128]{0,1,2:T(8,128)(2,1)} %copy-done.2) | copy-start | bytes 3145732
  293.1 14.8 %all-to-all-start.3 = ((bf16[256,4,4,32]{0,3,2,1:T(8,128)(2,1)}), bf16[256,4,4,32]{0,3,2,1:T(8,128)(2,1)S(1)}, u32[]{:S(2)}, u32[]{:S(2)}) async-start(bf16[256,4,4,32]{0,3,2,1:T(8,128)(2,1)} %copy.88), calls=%async_computation.3 | async-start | bytes 524288 | tf_op jit(solution)/shard_map/all_to_all | solution.py:28
  299.6 297.9 %all-reduce.6.cloned.1.call-start = ((), (), s32[]{:S(2)}) async-start(), calls=%async_computation.16 | async-start | bytes 524288 | tf_op jit(solution)/shard_map/psum | solution.py:164
  300.4 7.5 %copy-start.10 = (bf16[256,512]{0,1:T(8,128)(2,1)S(1)}, bf16[256,512]{0,1:T(8,128)(2,1)}, u32[]{:S(2)}) copy-start(bf16[256,512]{0,1:T(8,128)(2,1)} %copy.99) | copy-start | bytes 786436
  302.9 297.7 %copy-start.5 = (bf16[256,4,4,128]{0,3,2,1:T(8,128)(2,1)S(1)}, bf16[256,4,4,128]{0,3,2,1:T(8,128)(2,1)}, u32[]{:S(2)}) copy-start(bf16[256,4,4,128]{0,3,2,1:T(8,128)(2,1)} %copy-done.4) | copy-start | bytes 3145732
  309.3 311.0 %reduce-scatter.15.cloned.1.call-start = ((), (), s32[]{:S(2)}) async-start(), calls=%async_computation.18 | async-start | bytes 393216 | tf_op jit(solution)/shard_map/reduce_scatter | solution.py:40
  317.0 326.5 %reduce-scatter.11.cloned.1.call-start = ((), (), s32[]{:S(2)}) async-start(), calls=%async_computation.15 | async-start | bytes 393216 | tf_op jit(solution)/shard_map/reduce_scatter | solution.py:40
  (4 other events, 6.4 us)
Sparse Core Ops, SparseCore 0:
  13.7 42.2 all-gather.12
  58.1 22.8 all-gather.8
  83.0 37.5 all-gather.14
  122.5 22.7 all-gather.10
  217.5 54.1 all-reduce.7
  275.7 41.1 reduce-scatter.12
  319.8 43.4 reduce-scatter.8
  366.7 230.6 all-reduce.5
  601.0 19.2 reduce-scatter.14
  623.5 19.9 reduce-scatter.10
where the time goes:
time: 652 us; the launch traced here: 650 us
  waiting for transfers between devices  509 us (78%)
  blocking collectives  35.8 us (5%)
  local copies, waits for them, and re-layouts  33.3 us (5%)
  starting transfers between devices  31.5 us (5%)
  matrix products  23.7 us (4%)
  between operations  14.3 us (2%)
    psum x1, waiting for transfers between devices, on_device(): rights = lax.psum(rights, DP_AXES)  233 us
    all_gather x2, waiting for transfers between devices, dp_all_gather(): x = lax.all_gather(x, 'z', axis=row_axis, tiled=True)  75 us
    reduce_scatter x2, waiting for transfers between devices, dp_reduce_scatter(): x = lax.psum_scatter(x, 'z', scatter_dimension=row_axis, tiled=True)  53.9 us
    unnamed x11, waiting for transfers between devices  53.1 us
    all_to_all x4, waiting for transfers between devices, exchange(): shaped = lax.all_to_all(shaped, 'yhi', 1, 1, tiled=True)  40.3 us
    reduce_scatter x2, waiting for transfers between devices, dp_reduce_scatter(): x = lax.psum_scatter(x, 'ylo', scatter_dimension=row_axis + 1, tiled=True)  39.8 us
    all_to_all x2, blocking collectives, exchange(): shaped = lax.all_to_all(shaped, 'x', 2, 2, tiled=True)  24.2 us
    all_to_all x4, starting transfers between devices, exchange(): shaped = lax.all_to_all(shaped, 'yhi', 1, 1, tiled=True)  23.7 us
  transfers between devices with their start and end apart: 16, of which 14 were waited for; matrix products, arithmetic and copies ran while one was open for 7% of the time, Pallas kernels for 0%

commit v1 on v0

--- a/solution.py
+++ b/solution.py
@@ -161,7 +161,7 @@
         0,
     ).transpose(1, 0, 2)
     rights = jnp.concatenate([right_up_term, right_down_term], axis=0)
-    rights = lax.psum(rights, DP_AXES)
+    rights = jnp.sum(lax.all_gather(rights, DP_AXES), axis=0)
     grad_up_right = rights[:group_up]
     grad_down_right = rights[group_up:]
     return (layer_out, grad_tokens, grad_up_left, grad_up_right, grad_down_left, grad_down_right)

time: 652 us -> 653 us (level)
  other arithmetic: 2.13 us -> 17.5 us
  waiting for transfers between devices: 509 us -> 498 us
    psum x1 -> x0, waiting for transfers between devices: 233 us -> none  [on_device(): rights = lax.psum(rights, DP_AXES)]
    all_gather x0 -> x1, waiting for transfers between devices: none -> 230 us  [on_device(): rights = jnp.sum(lax.all_gather(rights, DP_AXES), axis=0)]
    reduce_sum x0 -> x1, other arithmetic: none -> 14.9 us  [on_device(): rights = jnp.sum(lax.all_gather(rights, DP_AXES), axis=0)]
    reduce_scatter x2, waiting for transfers between devices: 39.8 us -> 29.4 us  [dp_reduce_scatter(): x = lax.psum_scatter(x, 'ylo', scatter_dimension=row_axis + 1, tiled=True)]
    all_to_all x4, waiting for transfers between devices: 40.3 us -> 47.1 us  [exchange(): shaped = lax.all_to_all(shaped, 'yhi', 1, 1, tiled=True)]
    unnamed x29 -> x31, local copies, waits for them, and re-layouts: 14.7 us -> 15.7 us
  transfers between devices with their start and end apart: 16 -> 16, of which waited for: 14 -> 14; matrix products, arithmetic and copies ran while one was open for 7% -> 8% of each run, Pallas kernels for 0% -> 0%
where the time goes in v1:
time: 653 us; the launch traced here: 652 us
  waiting for transfers between devices  498 us (76%)
  blocking collectives  35.8 us (5%)
  starting transfers between devices  31.5 us (5%)
  local copies, waits for them, and re-layouts  30.6 us (5%)
  matrix products  23.7 us (4%)
  other arithmetic  17.5 us (3%)
  between operations  14.4 us (2%)
    all_gather x1, waiting for transfers between devices, on_device(): rights = jnp.sum(lax.all_gather(rights, DP_AXES), axis=0)  230 us
    all_gather x2, waiting for transfers between devices, dp_all_gather(): x = lax.all_gather(x, 'z', axis=row_axis, tiled=True)  75 us
    reduce_scatter x2, waiting for transfers between devices, dp_reduce_scatter(): x = lax.psum_scatter(x, 'z', scatter_dimension=row_axis, tiled=True)  53.6 us
    unnamed x11, waiting for transfers between devices  48.5 us
    all_to_all x4, waiting for transfers between devices, exchange(): shaped = lax.all_to_all(shaped, 'yhi', 1, 1, tiled=True)  47.1 us
    reduce_scatter x2, waiting for transfers between devices, dp_reduce_scatter(): x = lax.psum_scatter(x, 'ylo', scatter_dimension=row_axis + 1, tiled=True)  29.4 us
    all_to_all x2, blocking collectives, exchange(): shaped = lax.all_to_all(shaped, 'x', 2, 2, tiled=True)  24.2 us
    all_to_all x4, starting transfers between devices, exchange(): shaped = lax.all_to_all(shaped, 'yhi', 1, 1, tiled=True)  23.7 us
  transfers between devices with their start and end apart: 16, of which 14 were waited for; matrix products, arithmetic and copies ran while one was open for 8% of the time, Pallas kernels for 0%

profile of v1, /device:TPU:1, one launch (start us, length us, event | category | flops | bytes accessed | tf_op | source)
XLA Modules:
  0.0 651.8 jit_solution(788091459115869922)
XLA Ops:
  7.2 6.3 all-gather
  13.6 42.4 %all-gather.15.cloned.1.call-done = bf16[16,16,2048]{2,1,0:T(8,128)(2,1)} async-done(((bf16[2,16,2048]{2,1,0:T(8,128)(2,1)}), bf16[16,16,2048]{2,1,0:T(8,128)(2,1)}) %all-gather.15.cloned.1.call-update) | async-done | bytes 1048592 | tf_op jit(solution)/shard_map/all_gather | solution.py:49
  56.1 5.3 all-gather.2
  70.8 10.1 %all-gather.11.cloned.1.call-done = bf16[1,8,2,2,16,2048]{5,4,3,2,1,0:T(8,128)(2,1)} async-done(((bf16[1,8,2,1,16,2048]{5,4,3,2,1,0:T(8,128)(2,1)}), bf16[1,8,2,2,16,2048]{5,4,3,2,1,0:T(8,128)(2,1)}) %all-gather.11.cloned.1.call-update) | async-done | bytes 2097168 | tf_op jit(solution)/shard_map/all_gather | solution.py:50
  87.9 32.6 %all-gather.17.cloned.1.call-done = bf16[16,64,512]{2,1,0:T(8,128)(2,1)} async-done(((bf16[2,64,512]{2,1,0:T(8,128)(2,1)}), bf16[16,64,512]{2,1,0:T(8,128)(2,1)}) %all-gather.17.cloned.1.call-update) | async-done | bytes 1048592 | tf_op jit(solution)/shard_map/all_gather | solution.py:49
  121.3 6.5 all-to-all-start.5
  128.8 6.9 %all-to-all-done.5 = bf16[256,4,4,32]{0,3,2,1:T(8,128)(2,1)S(1)} async-done(((bf16[256,4,4,32]{0,3,2,1:T(8,128)(2,1)}), bf16[256,4,4,32]{0,3,2,1:T(8,128)(2,1)S(1)}, u32[]{:S(2)}, u32[]{:S(2)}) %all-to-all-start.5) | async-done | bytes 262176 | tf_op jit(solution)/shard_map/all_to_all | solution.py:28
  135.7 4.2 all-to-all-start.1
  147.6 18.1 %all-to-all-done.1 = bf16[256,4,4,128]{0,3,2,1:T(8,128)(2,1)} async-done(((bf16[256,4,4,128]{0,3,2,1:T(8,128)(2,1)}), bf16[256,4,4,128]{0,3,2,1:T(8,128)(2,1)}, u32[]{:S(2)}, u32[]{:S(2)}) %all-to-all-start.1) | async-done | bytes 1048608 | tf_op jit(solution)/shard_map/all_to_all | solution.py:28
  165.7 4.5 fusion.7
  172.3 15.0 %all_to_all.40 = bf16[256,4,4,128]{0,3,1,2:T(8,128)(2,1)S(1)} all-to-all(bf16[256,4,4,128]{0,3,1,2:T(8,128)(2,1)S(1)} %copy.123), channel_id=1, replica_groups=mesh['z'=8,'ylo'=2,'core'=2,'yhi'=4,'x'=4] {'x'}, dimensions={2} | all-to-all | bytes 2097152 | tf_op jit(solution)/shard_map/all_to_all | solution.py:27
  188.3 6.5 all-to-all-start.7
  198.9 5.4 copy.129
  204.3 15.9 %all-to-all-done.7 = bf16[256,4,4,128]{0,3,2,1:T(8,128)(2,1)S(1)} async-done(((bf16[256,4,4,128]{0,3,2,1:T(8,128)(2,1)}), bf16[256,4,4,128]{0,3,2,1:T(8,128)(2,1)S(1)}, u32[]{:S(2)}, u32[]{:S(2)}) %all-to-all-start.7) | async-done | bytes 1048608 | tf_op jit(solution)/shard_map/all_to_all | solution.py:28
  224.2 48.3 %all-reduce.5.cloned.1.call-done = (f32[8,2,2,16,1,2048]{5,3,4,2,1,0:T(8,128)}, f32[8,2,2,64,1,512]{5,3,2,1,0,4:T(8,128)}) async-done(((f32[8,2,2,16,1,2048]{5,3,4,2,1,0:T(8,128)}, f32[8,2,2,64,1,512]{5,3,2,1,0,4:T(8,128)}), (f32[8,2,2,16,1,2048]{5,3,4,2,1,0:T(8,128)}, f32[8,2,2,64,1,512]{5,3,2,1,0,4:T(8,128)})) %all-reduce.5.cloned.1.call-update) | async-done | bytes 8388624
  284.0 9.2 %all_to_all.41 = bf16[256,4,4,32]{0,3,1,2:T(8,128)(2,1)S(1)} all-to-all(bf16[256,4,4,32]{0,3,1,2:T(8,128)(2,1)S(1)} %copy.115), channel_id=1, replica_groups=mesh['z'=8,'ylo'=2,'core'=2,'yhi'=4,'x'=4] {'x'}, dimensions={2} | all-to-all | bytes 524288 | tf_op jit(solution)/shard_map/all_to_all | solution.py:27
  293.9 6.4 all-to-all-start.3
  302.5 6.2 all-to-all-done.3
  310.4 7.4 %reduce-scatter.13.cloned.1.call-done = f32[1,2,1,64,1,512]{5,3,2,1,0,4:T(8,128)} async-done(((f32[8,2,1,64,1,512]{5,3,2,1,0,4:T(8,128)}), f32[1,2,1,64,1,512]{5,3,2,1,0,4:T(8,128)}) %reduce-scatter.13.cloned.1.call-update) | async-done | bytes 262160 | tf_op jit(solution)/shard_map/reduce_scatter | solution.py:39
  317.8 46.2 %reduce-scatter.9.cloned.1.call-done = f32[1,2,1,16,1,2048]{5,3,4,2,1,0:T(8,128)} async-done(((f32[8,2,1,16,1,2048]{5,3,4,2,1,0:T(8,128)}), f32[1,2,1,16,1,2048]{5,3,4,2,1,0:T(8,128)}) %reduce-scatter.9.cloned.1.call-update) | async-done | bytes 262160 | tf_op jit(solution)/shard_map/reduce_scatter | solution.py:39
  368.2 230.4 %all-gather.19.cloned.1.call-done = f32[5120,16,16]{2,1,0:T(8,128)} async-done(((f32[160,16,16]{2,1,0:T(8,128)}), f32[5120,16,16]{2,1,0:T(8,128)}) %all-gather.19.cloned.1.call-update) | async-done | bytes 5242896 | tf_op jit(solution)/shard_map/all_gather | solution.py:164
  598.6 14.9 %reduce_sum.9 = f32[160,16,16]{2,1,0:T(8,128)S(1)} reduce(f32[32,160,16,16]{3,2,1,0:T(8,128)} %bitcast.116, f32[]{:T(128)} %constant.5.clone.1), dimensions={0}, to_apply=%region_3.0 | reduce | flops 1269760 | bytes 5406724 | tf_op jit(solution)/shard_map/reduce_sum | solution.py:164
  615.5 6.0 reduce-scatter.15.cloned.1.call-done
  621.5 23.4 %reduce-scatter.11.cloned.1.call-done = f32[1,1,1,16,1,2048]{5,3,4,2,1,0:T(8,128)} async-done(((f32[1,2,1,16,1,2048]{5,3,4,2,1,0:T(8,128)}), f32[1,1,1,16,1,2048]{5,3,4,2,1,0:T(8,128)}) %reduce-scatter.11.cloned.1.call-update) | async-done | bytes 131088 | tf_op jit(solution)/shard_map/reduce_scatter | solution.py:40
  (85 shorter events, 59.1 us)
Async XLA Ops:
  7.2 73.8 %copy-start = (bf16[256,512]{1,0:T(8,128)(2,1)S(1)}, bf16[256,512]{1,0:T(8,128)(2,1)}, u32[]{:S(2)}) copy-start(bf16[256,512]{1,0:T(8,128)(2,1)} %param.6) | copy-start | bytes 786436
  7.2 48.8 %all-gather.15.cloned.1.call-start = ((), (), s32[]{:S(2)}) async-start(), calls=%async_computation.18 | async-start | bytes 1179648 | tf_op jit(solution)/shard_map/all_gather | solution.py:49
  13.6 67.3 %all-gather.11.cloned.1.call-start = ((), (), s32[]{:S(2)}) async-start(), calls=%async_computation.12 | async-start | bytes 3145728 | tf_op jit(solution)/shard_map/all_gather | solution.py:50
  56.0 64.5 %all-gather.17.cloned.1.call-start = ((), (), s32[]{:S(2)}) async-start(), calls=%async_computation.19 | async-start | bytes 1179648 | tf_op jit(solution)/shard_map/all_gather | solution.py:49
  62.3 3.5 copy-start.10
  66.9 17.5 %all-to-all-start.4 = ((bf16[256,4,4,32]{0,3,1,2:T(8,128)(2,1)}), bf16[256,4,4,32]{0,3,1,2:T(8,128)(2,1)S(1)}, u32[]{:S(2)}, u32[]{:S(2)}) async-start(bf16[256,4,4,32]{0,3,1,2:T(8,128)(2,1)} %copy.118), calls=%async_computation.4 | async-start | bytes 524288 | tf_op jit(solution)/shard_map/all_to_all | solution.py:27
  84.4 37.0 %all-to-all-start = ((bf16[256,4,4,128]{0,3,1,2:T(8,128)(2,1)}), bf16[256,4,4,128]{0,3,1,2:T(8,128)(2,1)S(1)}, u32[]{:S(2)}, u32[]{:S(2)}) async-start(bf16[256,4,4,128]{0,3,1,2:T(8,128)(2,1)} %copy.109), calls=%async_computation | async-start | bytes 2097152 | tf_op jit(solution)/shard_map/all_to_all | solution.py:27
  87.9 57.4 %all-gather.13.cloned.1.call-start = ((), (), s32[]{:S(2)}) async-start(), calls=%async_computation.13 | async-start | bytes 3145728 | tf_op jit(solution)/shard_map/all_gather | solution.py:50
  121.3 14.4 %all-to-all-start.5 = ((bf16[256,4,4,32]{0,3,2,1:T(8,128)(2,1)}), bf16[256,4,4,32]{0,3,2,1:T(8,128)(2,1)S(1)}, u32[]{:S(2)}, u32[]{:S(2)}) async-start(bf16[256,4,4,32]{0,3,2,1:T(8,128)(2,1)} %copy.119), calls=%async_computation.5 | async-start | bytes 524288 | tf_op jit(solution)/shard_map/all_to_all | solution.py:28
  127.8 12.2 %copy-start.11 = (bf16[128,16,16]{0,2,1:T(8,128)(2,1)S(1)}, bf16[128,16,16]{0,2,1:T(8,128)(2,1)}, u32[]{:S(2)}) copy-start(bf16[128,16,16]{0,2,1:T(8,128)(2,1)} %param.8) | copy-start | bytes 196612
  135.7 30.0 %all-to-all-start.1 = ((bf16[256,4,4,128]{0,3,2,1:T(8,128)(2,1)}), bf16[256,4,4,128]{0,3,2,1:T(8,128)(2,1)}, u32[]{:S(2)}, u32[]{:S(2)}) async-start(bf16[256,4,4,128]{0,3,2,1:T(8,128)(2,1)} %copy.110), calls=%async_computation.1 | async-start | bytes 2097152 | tf_op jit(solution)/shard_map/all_to_all | solution.py:28
  165.7 5.5 copy-start.8
  187.3 7.5 %copy-start.9 = (bf16[256,16,128]{0,1,2:T(8,128)(2,1)S(1)}, bf16[256,16,128]{0,1,2:T(8,128)(2,1)}, u32[]{:S(2)}) copy-start(bf16[256,16,128]{0,1,2:T(8,128)(2,1)} %get-tuple-element.33) | copy-start | bytes 3145732
  188.3 31.9 %all-to-all-start.7 = ((bf16[256,4,4,128]{0,3,2,1:T(8,128)(2,1)}), bf16[256,4,4,128]{0,3,2,1:T(8,128)(2,1)S(1)}, u32[]{:S(2)}, u32[]{:S(2)}) async-start(bf16[256,4,4,128]{0,3,2,1:T(8,128)(2,1)} %copy.124), calls=%async_computation.7 | async-start | bytes 2097152 | tf_op jit(solution)/shard_map/all_to_all | solution.py:28
  194.8 77.7 %all-reduce.5.cloned.1.call-start = ((), (), s32[]{:S(2)}) async-start(), calls=%async_computation.21 | async-start | bytes 16777216
  222.9 94.8 %reduce-scatter.13.cloned.1.call-start = ((), (), s32[]{:S(2)}) async-start(), calls=%async_computation.16 | async-start | bytes 2359296 | tf_op jit(solution)/shard_map/reduce_scatter | solution.py:39
  276.4 87.7 %reduce-scatter.9.cloned.1.call-start = ((), (), s32[]{:S(2)}) async-start(), calls=%async_computation.14 | async-start | bytes 2359296 | tf_op jit(solution)/shard_map/reduce_scatter | solution.py:39
  283.8 16.7 %copy-start.4 = (bf16[256,16,128]{0,1,2:T(8,128)(2,1)S(1)}, bf16[256,16,128]{0,1,2:T(8,128)(2,1)}, u32[]{:S(2)}) copy-start(bf16[256,16,128]{0,1,2:T(8,128)(2,1)} %copy-done.3) | copy-start | bytes 3145732
  293.9 14.8 %all-to-all-start.3 = ((bf16[256,4,4,32]{0,3,2,1:T(8,128)(2,1)}), bf16[256,4,4,32]{0,3,2,1:T(8,128)(2,1)S(1)}, u32[]{:S(2)}, u32[]{:S(2)}) async-start(bf16[256,4,4,32]{0,3,2,1:T(8,128)(2,1)} %copy.116), calls=%async_computation.3 | async-start | bytes 524288 | tf_op jit(solution)/shard_map/all_to_all | solution.py:28
  300.4 298.2 %all-gather.19.cloned.1.call-start = ((), (), s32[]{:S(2)}) async-start(), calls=%async_computation.20 | async-start | bytes 43253760 | tf_op jit(solution)/shard_map/all_gather | solution.py:164
  310.3 54.9 %copy-start.6 = (bf16[256,4,4,128]{0,3,2,1:T(8,128)(2,1)S(1)}, bf16[256,4,4,128]{0,3,2,1:T(8,128)(2,1)}, u32[]{:S(2)}) copy-start(bf16[256,4,4,128]{0,3,2,1:T(8,128)(2,1)} %copy-done.5) | copy-start | bytes 3145732
  310.3 311.2 %reduce-scatter.15.cloned.1.call-start = ((), (), s32[]{:S(2)}) async-start(), calls=%async_computation.17 | async-start | bytes 393216 | tf_op jit(solution)/shard_map/reduce_scatter | solution.py:40
  317.8 327.1 %reduce-scatter.11.cloned.1.call-start = ((), (), s32[]{:S(2)}) async-start(), calls=%async_computation.15 | async-start | bytes 393216 | tf_op jit(solution)/shard_map/reduce_scatter | solution.py:40
  598.6 46.3 %copy-start.1 = (bf16[256,512]{1,0:T(8,128)(2,1)S(1)}, bf16[256,512]{1,0:T(8,128)(2,1)}, u32[]{:S(2)}) copy-start(bf16[256,512]{1,0:T(8,128)(2,1)} %param.6) | copy-start | bytes 786436
  (4 other events, 6.2 us)
Sparse Core Ops, SparseCore 0:
  13.7 42.2 all-gather.14
  58.1 22.8 all-gather.10
  83.0 37.5 all-gather.16
  122.5 22.7 all-gather.12
  223.0 49.4 all-reduce.4
  276.5 41.1 reduce-scatter.12
  320.6 43.4 reduce-scatter.8
  366.2 232.3 all-gather.18
  601.9 19.5 reduce-scatter.14
  624.9 19.9 reduce-scatter.10
